TPU v7x, 256 devices: a whole 4x4x8 slice. The times are simulated.
256 devices in a mesh: section: 16 (over y_lo, x, core), expert: 16 (over z, y_hi).
Axes of the slice: x: 4, y: 4 (y_hi: 2, y_lo: 2; y = y_hi * 2 + y_lo), z: 8, core: 2. Of those that a mesh axis runs over, the one named last changes fastest.
Arguments:
- activations: bfloat16 [16384, 8192], P('section', 'expert'), may hold values from -12 to 12
- modality: int32 [16384], P('section'), may hold values from 0 to 1
- selected: int32 [16, 256], P('section'), may hold values from 0 to 1023, as said below
- routes: int32 [4096, 1], P('section'), may hold values from 0 to 15, as said below
- norm_gain: float32 [2, 8192], P(None, 'expert'), may hold values from 0.1 to 1.9
- router: float32 [8192], P('expert'), may hold values from -0.0625 to 0.0625
- gate_w: bfloat16 [16, 3072, 8192], P('expert', 'section'), may hold values from -0.0625 to 0.0625
- up_w: bfloat16 [16, 3072, 8192], P('expert', 'section'), may hold values from -0.0625 to 0.0625
- down_w: bfloat16 [16, 3072, 8192], P('expert', 'section'), may hold values from -0.21875 to 0.21875
Outputs:
- block_out: bfloat16 [16384, 8192], P('section', 'expert')
Inputs may be any that keep to these rules, and one draw needn't show every extreme that they name: Each row of selected lists 256 different positions in rising order, the first and the last position among them. `routes`: among the 256 rows of one section group no expert is named more than 24 times, and some expert exactly 24 times; the entry for selected[s, j] is below 8 if that token's modality is 0, and 8 or more if it is 1.
All inputs are finite; a program needn't handle non-finite values.
Results may differ from a plain program's by a relative error of at most 0.0075.
Values may be sent and summed in bfloat16 or wider, within the bound.
No kernel may reach another device: no remote copies, remote signals or barrier semaphores. Data moves between devices by JAX's collectives and lax.ppermute only.
A program may use at most 128 MiB of HBM per device.

v0:
```python
import jax
import jax.numpy as jnp
from jax import lax
from jax.sharding import PartitionSpec as P

EPS = 1e-05
SECTION = ("chip", "core")


def passed_along(block, axis, distance):
    names = axis if isinstance(axis, tuple) else (axis,)
    count = 1
    for name in names:
        count *= lax.axis_size(name)
    route = [((i - distance) % count, i) for i in range(count)]
    return lax.ppermute(block, axis, route)


def feature_product(block, weight):
    return lax.dot_general(
        block, weight, (((1,), (1,)), ((), ())), preferred_element_type=jnp.float32
    )


def body(activations, modality, selected, routes, norm_gain, router, gate_w, up_w, down_w):
    n_chip = lax.axis_size("chip")
    n_core = lax.axis_size("core")
    n_section = n_chip * n_core
    sel_count = selected.shape[1]
    expert_count = lax.axis_size("expert") * gate_w.shape[0]
    capacity = max(2, 3 * sel_count // (2 * expert_count))
    groups = n_section
    sel_next = passed_along(selected, SECTION, -1)[0]
    routes_next = passed_along(routes, SECTION, -1)[:, 0]
    rows = activations[sel_next]
    both = jnp.stack([routes_next, routes[:, 0]], axis=1)
    onehot = (both[:, :, None] == jnp.arange(expert_count, dtype=jnp.int32)[None, None, :]).astype(
        jnp.int32
    )
    slots = jnp.sum((jnp.cumsum(onehot, axis=0) - 1) * onehot, axis=2)
    targets = both * capacity + slots
    target = targets[:, 0]
    position = targets[:, 1]
    feature_width = rows.shape[1]
    n_exp_dev = lax.axis_size("expert")
    local_width = router.shape[0]
    tables = jnp.concatenate([norm_gain, router[None, :]], axis=0)
    table_count = tables.shape[0]
    parts = []
    rest = tables
    for _ in range(3):
        piece = rest.astype(jnp.bfloat16)
        parts.append(piece)
        rest = rest - piece.astype(jnp.float32)
    sources = jnp.concatenate([rows] + parts, axis=0)
    table_rows = 2
    coded_rows = 3 * table_rows
    span = capacity + -(-coded_rows // 8) * 8
    slot_of_row = jnp.arange(expert_count * span, dtype=jnp.int32)
    row_expert = slot_of_row // span
    row_slot = slot_of_row % span
    row_kind = (row_expert >= expert_count // 2).astype(jnp.int32)
    coded_index = row_slot - capacity
    part_index = coded_index // table_rows
    table_index = jnp.where(coded_index % table_rows == 0, row_kind, table_count - 1)
    wanted = jnp.where(row_slot < capacity, row_expert * capacity + row_slot, -1)
    token_hit = target[None, :] == wanted[:, None]
    table_source = jnp.where(
        (coded_index >= 0) & (coded_index < coded_rows), part_index * table_count + table_index, -1
    )
    table_hit = table_source[:, None] == jnp.arange(3 * table_count, dtype=jnp.int32)[None, :]
    placing = jnp.concatenate([token_hit, table_hit], axis=1).astype(jnp.bfloat16)
    buffer = jnp.dot(placing, sources, preferred_element_type=jnp.float32).astype(jnp.bfloat16)
    buffer = buffer.reshape(expert_count, span, feature_width)
    mine = lax.all_to_all(buffer, "expert", split_axis=0, concat_axis=2, tiled=True)[0]
    coded = mine[capacity : capacity + coded_rows].astype(jnp.float32)
    coded = coded.reshape(3, table_rows, mine.shape[1])
    tables = coded[0] + coded[1] + coded[2]
    mine = mine[:capacity]
    gains = tables[0]
    router_all = tables[1]
    picked = mine.astype(jnp.float32)
    d = picked.shape[1]
    scale = lax.rsqrt(jnp.sum(picked * picked, axis=1) / d + EPS)
    normed = (picked * scale[:, None] * gains[None, :]).astype(jnp.bfloat16)
    score = jax.nn.sigmoid(scale * jnp.sum(picked * gains[None, :] * router_all[None, :], axis=1))
    score_home = passed_along(score, SECTION, 1)
    block = lax.all_gather(normed, SECTION, axis=0, tiled=True)
    stacked = jnp.concatenate([gate_w[0], up_w[0]], axis=0)
    block, score_home, leaving, stacked = lax.optimization_barrier(
        (block, score_home, activations, stacked)
    )
    arrived = passed_along(leaving, SECTION, 1)
    both_products = feature_product(block, stacked)
    hidden_units = gate_w.shape[1]
    gate = both_products[:, :hidden_units]
    upper = both_products[:, hidden_units:]
    hidden = (jax.nn.silu(gate) * upper).astype(jnp.bfloat16)
    hidden_width = hidden.shape[1]
    order = []
    for core in range(n_core):
        for chip in range(n_chip):
            order.append((chip * n_core + core - 1) % n_section)
    hidden = jnp.take(
        hidden.reshape(groups, capacity, hidden_width), jnp.array(order, jnp.int32), axis=0
    ).reshape(groups * capacity, hidden_width)
    hidden = hidden.reshape(n_core, n_chip * capacity, hidden_width)
    core = lax.axis_index("core")

    def down_part(rows):
        part = jnp.dot(rows, down_w[0], preferred_element_type=jnp.float32)
        return (
            lax.optimization_barrier(part.astype(jnp.bfloat16))
            .astype(jnp.float32)
            .astype(jnp.bfloat16)
        )

    give = down_part(lax.dynamic_index_in_dim(hidden, 1 - core, axis=0, keepdims=False))
    taken = lax.ppermute(give, "core", [(0, 1), (1, 0)])
    keep = down_part(lax.dynamic_index_in_dim(hidden, core, axis=0, keepdims=False))
    pair = (keep.astype(jnp.float32) + taken.astype(jnp.float32)).astype(jnp.bfloat16)
    summed = lax.psum_scatter(pair, "chip", scatter_dimension=0, tiled=True)
    update_rows = (score_home[:, None] * summed.astype(jnp.float32)).astype(jnp.bfloat16)
    outgoing = update_rows.reshape(capacity, n_exp_dev, local_width).transpose(1, 0, 2)
    back = lax.all_to_all(outgoing, "expert", split_axis=0, concat_axis=0, tiled=True)
    flat_back = back.reshape(expert_count * capacity, local_width)
    picks = selected[0]
    token_count = arrived.shape[0]
    source = jnp.full((token_count,), -1, jnp.int32).at[picks].set(position)
    spread = (
        source[:, None] == jnp.arange(expert_count * capacity, dtype=jnp.int32)[None, :]
    ).astype(jnp.bfloat16)
    update = jnp.dot(spread, flat_back, preferred_element_type=jnp.float32)
    return (arrived.astype(jnp.float32) + update).astype(jnp.bfloat16)


def solution(mesh):
    n_section, n_expert = mesh.devices.shape
    split = jax.sharding.Mesh(
        mesh.devices.reshape(n_section // 2, 2, n_expert), ("chip", "core", "expert")
    )
    placed = (
        P(SECTION, "expert"),
        P(SECTION),
        P(SECTION, None),
        P(SECTION, None),
        P(None, "expert"),
        P("expert"),
        P("expert", SECTION, None),
        P("expert", SECTION, None),
        P("expert", SECTION, None),
    )
    return jax.shard_map(
        body, mesh=split, in_specs=placed, out_specs=P(SECTION, "expert"), check_vma=False
    )
```

profile of v0, /device:TPU:6, one launch (start us, length us, event | category | flops | bytes accessed | tf_op | source)
XLA Modules:
  0.0 195.6 jit_solution(17597508050167331478)
XLA Ops:
  6.5 0.0 copy-start
  6.5 0.0 all-gather.2.cloned.1.call-start
  6.5 0.3 collective-permute-start
  6.8 0.7 collective-permute-start.1
  7.5 0.7 fusion.27
  8.2 0.7 fusion.22
  8.9 0.8 iota_compare_fusion.2
  9.7 0.0 collective-permute-done
  9.7 0.7 pad_add_fusion
  10.4 1.2 reduce-window.6
  11.6 0.1 slice.66
  11.6 0.1 copy.22
  11.8 0.1 fusion.20
  11.9 0.7 multiply_add_fusion
  12.6 0.5 fusion.49
  13.1 0.0 collective-permute-done.1
  13.2 0.1 broadcast_compare_fusion
  13.3 2.6 %gather_fusion = bf16[256,512]{1,0:T(8,128)(2,1)S(1)} fusion(bf16[1024,512]{1,0:T(8,128)(2,1)} %param.10, s32[1024]{0:T(1024)S(1)} %pad_clamp_fusion.1), kind=kCustom, calls=%fused_computation | custom fusion | bytes 525312 | tf_op jit(solution)/shard_map/gather | solution.py:35
  15.9 1.3 convolution_convert_fusion.2
  17.2 30.0 %all_to_all.20 = bf16[16,32,512]{2,1,0:T(8,128)(2,1)S(1)} all-to-all(bf16[16,32,512]{2,1,0:T(8,128)(2,1)S(1)} %bitcast.81), channel_id=1, replica_groups=mesh['chip'=8,'core'=2,'expert'=16] {'expert'}, dimensions={0} | all-to-all | bytes 1048576 | tf_op jit(solution)/shard_map/all_to_all | solution.py:75
  47.2 0.0 copy-start.2
  47.2 0.1 fusion.50
  47.3 0.1 slice_add_fusion
  47.4 0.1 fusion.48
  47.4 0.1 copy.32
  47.5 0.3 multiply_reduce_fusion
  47.8 0.9 multiply_convert_fusion.1
  48.7 0.0 all-gather.2.cloned.1.call-update
  48.7 0.0 reduce-scatter.2.cloned.1.call-start
  48.8 0.0 copy-done.2
  48.8 6.2 %pad_maximum_fusion = bf16[384,8192]{1,0:T(8,128)(2,1)} fusion(bf16[192,8192]{1,0:T(8,128)(2,1)} %bitcast.73, bf16[192,8192]{1,0:T(8,128)(2,1)} %bitcast.74), kind=kLoop, calls=%fused_computation.5 | loop fusion | flops 12582912 | bytes 12582912 | tf_op jit(solution)/shard_map/concatenate | solution.py:89
  55.0 1.6 collective-permute-start.2
  56.6 1.4 collective-permute-done.2
  58.0 31.2 %all-gather.2.cloned.1.call-done = bf16[384,8192]{1,0:T(8,128)(2,1)} async-done(((bf16[24,8192]{1,0:T(8,128)(2,1)}), bf16[384,8192]{1,0:T(8,128)(2,1)}) %all-gather.2.cloned.1.call-update) | async-done | bytes 6291472 | tf_op jit(solution)/shard_map/all_gather | solution.py:88
  89.2 8.2 %fusion.51 = f32[384,384]{0,1:T(8,128)S(1)} fusion(bf16[384,8192]{1,0:T(8,128)(2,1)} %all-gather.2.cloned.1.call-done, bf16[384,8192]{1,0:T(8,128)(2,1)} %pad_maximum_fusion), kind=kOutput, calls=%fused_computation.100 | convolution fusion | flops 2415919104 | bytes 13172736 | tf_op jit(solution)/shard_map/dot_general | solution.py:20
  97.4 0.1 fusion.7
  97.5 0.1 copy.26
  97.7 0.6 gather_fusion.1
  98.2 0.0 copy-done
  98.3 2.6 %convolution_convert_fusion = bf16[192,8192]{1,0:T(8,128)(2,1)} fusion(bf16[1,192,8192]{2,1,0:T(8,128)(2,1)S(1)} %copy-done, bf16[2,192,192]{2,1,0:T(8,128)(2,1)S(1)} %bitcast.78, s32[]{:T(128)S(6)} %select_n.116), kind=kOutput, calls=%fused_computation.3 | convolution fusion | flops 605552640 | bytes 6389764 | tf_op jit(solution)/shard_map/dot_general | solution.py:111
  100.9 0.2 collective-permute-start.4
  101.1 1.0 convolution_convert_fusion.1
  102.1 4.8 %collective-permute-done.4 = bf16[192,8192]{1,0:T(8,128)(2,1)} collective-permute-done((bf16[192,8192]{1,0:T(8,128)(2,1)}, bf16[192,8192]{1,0:T(8,128)(2,1)}, u32[]{:S(2)}, u32[]{:S(2)}) %collective-permute-start.4) | collective-permute-done | bytes 3145760 | tf_op jit(solution)/shard_map/ppermute | solution.py:119
  106.9 4.6 %add_convert_fusion = bf16[192,8192]{1,0:T(8,128)(2,1)} fusion(bf16[192,8192]{1,0:T(8,128)(2,1)} %collective-permute-done.4, bf16[192,8192]{1,0:T(8,128)(2,1)S(1)} %convolution_convert_fusion.1), kind=kLoop, calls=%fused_computation.6 | loop fusion | flops 6291456 | bytes 9437184 | tf_op jit(solution)/shard_map/convert_element_type | solution.py:121
  111.5 0.0 copy-start.1
  111.5 0.0 reduce-scatter.2.cloned.1.call-update
  111.5 0.5 collective-permute-start.3
  112.0 48.7 %reduce-scatter.2.cloned.1.call-done = bf16[24,8192]{1,0:T(8,128)(2,1)} async-done(((bf16[192,8192]{1,0:T(8,128)(2,1)}), bf16[24,8192]{1,0:T(8,128)(2,1)}) %reduce-scatter.2.cloned.1.call-update) | async-done | bytes 393232 | tf_op jit(solution)/shard_map/reduce_scatter | solution.py:122
  160.8 1.1 multiply_convert_fusion
  161.9 0.8 copy.38
  162.7 9.3 %all-to-all-start.1 = ((bf16[16,24,512]{2,1,0:T(8,128)(2,1)}), bf16[16,24,512]{2,1,0:T(8,128)(2,1)S(1)}, u32[]{:S(2)}, u32[]{:S(2)}) async-start(bf16[16,24,512]{2,1,0:T(8,128)(2,1)} %bitcast.76), calls=%async_computation.2 | async-start | bytes 786432 | tf_op jit(solution)/shard_map/all_to_all | solution.py:125
  172.0 0.0 copy-done.1
  172.0 1.6 scatter_custom_fusion
  173.6 11.9 %all-to-all-done.1 = bf16[16,24,512]{2,1,0:T(8,128)(2,1)S(1)} async-done(((bf16[16,24,512]{2,1,0:T(8,128)(2,1)}), bf16[16,24,512]{2,1,0:T(8,128)(2,1)S(1)}, u32[]{:S(2)}, u32[]{:S(2)}) %all-to-all-start.1) | async-done | bytes 393248 | tf_op jit(solution)/shard_map/all_to_all | solution.py:125
  185.5 0.8 fusion.2
  186.2 0.0 collective-permute-done.3
  186.2 2.6 %add_convert_fusion.1 = bf16[1024,512]{1,0:T(8,128)(2,1)} fusion(f32[1024,512]{1,0:T(8,128)S(1)} %fusion.2, bf16[1024,512]{1,0:T(8,128)(2,1)} %collective-permute-done.3), kind=kLoop, calls=%fused_computation.9 | loop fusion | flops 1572864 | bytes 4194304 | tf_op jit(solution)/shard_map/convert_element_type | solution.py:134
  (13 shorter events, 0.1 us)
Async XLA Ops:
  6.5 91.7 %copy-start = (bf16[1,192,8192]{2,1,0:T(8,128)(2,1)S(1)}, bf16[1,192,8192]{2,1,0:T(8,128)(2,1)}, u32[]{:S(2)}) copy-start(bf16[1,192,8192]{2,1,0:T(8,128)(2,1)} %param.17) | copy-start | bytes 9437188
  6.5 82.7 %all-gather.2.cloned.1.call-start = ((), (), s32[]{:S(2)}) async-start(), calls=%async_computation.3 | async-start | bytes 6684672 | tf_op jit(solution)/shard_map/all_gather | solution.py:88
  6.5 3.2 %collective-permute-start = (s32[256,1]{0,1:T(1,128)}, s32[256,1]{0,1:T(1,128)S(1)}, u32[]{:S(2)}, u32[]{:S(2)}) collective-permute-start(s32[256,1]{0,1:T(1,128)} %param.12), channel_id=1, source_target_pairs={{16,0},{32,16},{48,32},{64,48},{80,64},{96,80},{112,96},{128,112},... | collective-permute-start | bytes 3080 | tf_op jit(solution)/shard_map/ppermute | solution.py:16
  6.8 6.3 %collective-permute-start.1 = (s32[1,256]{1,0:T(1,128)}, s32[1,256]{1,0:T(1,128)S(1)}, u32[]{:S(2)}, u32[]{:S(2)}) collective-permute-start(s32[1,256]{1,0:T(1,128)} %param.11), channel_id=1, source_target_pairs={{16,0},{32,16},{48,32},{64,48},{80,64},{96,80},{112,96},{128,112},... | collective-permute-start | bytes 3080 | tf_op jit(solution)/shard_map/ppermute | solution.py:16
  47.2 1.6 copy-start.2
  48.7 112.0 %reduce-scatter.2.cloned.1.call-start = ((), (), s32[]{:S(2)}) async-start(), calls=%async_computation.4 | async-start | bytes 3538944 | tf_op jit(solution)/shard_map/reduce_scatter | solution.py:122
  55.0 3.0 %collective-permute-start.2 = (f32[24]{0:T(128)S(1)}, f32[24]{0:T(128)S(1)}, u32[]{:S(2)}, u32[]{:S(2)}) collective-permute-start(f32[24]{0:T(128)S(1)} %get-tuple-element.23), channel_id=1, source_target_pairs={{240,0},{0,16},{16,32},{32,48},{48,64},{64,80},{80,96},{96,112},{1... | collective-permute-start | bytes 296 | tf_op jit(solution)/shard_map/ppermute | solution.py:16
  100.9 6.0 %collective-permute-start.4 = (bf16[192,8192]{1,0:T(8,128)(2,1)}, bf16[192,8192]{1,0:T(8,128)(2,1)}, u32[]{:S(2)}, u32[]{:S(2)}) collective-permute-start(bf16[192,8192]{1,0:T(8,128)(2,1)} %convolution_convert_fusion), channel_id=1, source_target_pairs={{0,16},{16,0},{1,17},{17,1},{2,18},{18,2},{3,19},{19,3},{4,20},{20... | collective-permute-start | bytes 9437192 | tf_op jit(solution)/shard_map/ppermute | solution.py:119
  111.5 60.5 %copy-start.1 = (s32[1,256]{1,0:T(1,128)S(1)}, s32[1,256]{1,0:T(1,128)}, u32[]{:S(2)}) copy-start(s32[1,256]{1,0:T(1,128)} %param.11) | copy-start | bytes 3076
  111.5 74.7 %collective-permute-start.3 = (bf16[1024,512]{1,0:T(8,128)(2,1)}, bf16[1024,512]{1,0:T(8,128)(2,1)}, u32[]{:S(2)}, u32[]{:S(2)}) collective-permute-start(bf16[1024,512]{1,0:T(8,128)(2,1)} %param.10), channel_id=1, source_target_pairs={{240,0},{0,16},{16,32},{32,48},{48,64},{64,80},{80,96},{96,112},{1... | collective-permute-start | bytes 3145736 | tf_op jit(solution)/shard_map/ppermute | solution.py:16
  162.7 22.8 %all-to-all-start.1 = ((bf16[16,24,512]{2,1,0:T(8,128)(2,1)}), bf16[16,24,512]{2,1,0:T(8,128)(2,1)S(1)}, u32[]{:S(2)}, u32[]{:S(2)}) async-start(bf16[16,24,512]{2,1,0:T(8,128)(2,1)} %bitcast.76), calls=%async_computation.2 | async-start | bytes 786432 | tf_op jit(solution)/shard_map/all_to_all | solution.py:125
Sparse Core Ops, SparseCore 0:
  48.9 40.3 all-gather.1
  111.6 49.0 reduce-scatter.1
where the time goes:
time: 196 us
  waiting for transfers between devices  98 us (50%)
  blocking collectives  30 us (15%)
  other arithmetic  21 us (11%)
  matrix products  13.9 us (7%)
  between operations  13.6 us (7%)
  starting transfers between devices  12.6 us (6%)
  local copies, waits for them, and re-layouts  6.47 us (3%)
    reduce_scatter x1, waiting for transfers between devices, body(): summed = lax.psum_scatter(pair, 'chip', scatter_dimension=0, tiled=True)  48.7 us
    all_gather x1, waiting for transfers between devices, body(): block = lax.all_gather(normed, SECTION, axis=0, tiled=True)  31.2 us
    all_to_all x1, blocking collectives, body(): lax.all_to_all(buffer, 'expert', split_axis=0, concat_axis=2, tiled=True)[0]  30 us
    all_to_all x1, waiting for transfers between devices, body(): lax.all_to_all(outgoing, 'expert', split_axis=0, concat_axis=0, tiled=True)  11.9 us
    all_to_all x1, starting transfers between devices, body(): lax.all_to_all(outgoing, 'expert', split_axis=0, concat_axis=0, tiled=True)  9.31 us
    dot_general x1, matrix products, feature_product(): lax.dot_general(block, weight, (((1,), (1,)), ((), ())), preferred_elemen...  8.2 us
    concatenate x1, other arithmetic, body(): stacked = jnp.concatenate([gate_w[0], up_w[0]], axis=0)  6.21 us
    ppermute x1, waiting for transfers between devices, body(): taken = lax.ppermute(give, 'core', [(0, 1), (1, 0)])  4.77 us
  transfers between devices with their start and end apart: 8, of which 5 were waited for; matrix products, arithmetic and copies ran while one was open for 9% of the time, Pallas kernels for 0%

commit v1 on v0

--- a/solution.py
+++ b/solution.py
@@ -72,7 +72,12 @@
     placing = jnp.concatenate([token_hit, table_hit], axis=1).astype(jnp.bfloat16)
     buffer = jnp.dot(placing, sources, preferred_element_type=jnp.float32).astype(jnp.bfloat16)
     buffer = buffer.reshape(expert_count, span, feature_width)
-    mine = lax.all_to_all(buffer, "expert", split_axis=0, concat_axis=2, tiled=True)[0]
+    mine = jnp.concatenate(
+        lax.all_to_all(
+            jnp.stack(jnp.split(buffer, lax.axis_size("expert"), axis=0)), "expert", 0, 0
+        ),
+        axis=2,
+    )[0]
     coded = mine[capacity : capacity + coded_rows].astype(jnp.float32)
     coded = coded.reshape(3, table_rows, mine.shape[1])
     tables = coded[0] + coded[1] + coded[2]

time: 196 us -> 198 us (1.010)
  no operation moved by 1% of the time
where the time goes in v1:
time: 198 us; the launch traced here: 197 us
  waiting for transfers between devices  98.2 us (50%)
  blocking collectives  30.5 us (15%)
  other arithmetic  22.3 us (11%)
  matrix products  13.9 us (7%)
  between operations  13.7 us (7%)
  starting transfers between devices  12 us (6%)
  local copies, waits for them, and re-layouts  6.58 us (3%)
    reduce_scatter x1, waiting for transfers between devices, body(): summed = lax.psum_scatter(pair, 'chip', scatter_dimension=0, tiled=True)  48.7 us
    all_gather x1, waiting for transfers between devices, body(): block = lax.all_gather(normed, SECTION, axis=0, tiled=True)  30.8 us
    all_to_all x1, blocking collectives, body(): lax.all_to_all(jnp.stack(jnp.split(buffer, lax.axis_size('expert'), axis=...  30.5 us
    all_to_all x1, waiting for transfers between devices, body(): lax.all_to_all(outgoing, 'expert', split_axis=0, concat_axis=0, tiled=True)  11.9 us
    all_to_all x1, starting transfers between devices, body(): lax.all_to_all(outgoing, 'expert', split_axis=0, concat_axis=0, tiled=True)  9.3 us
    dot_general x1, matrix products, feature_product(): lax.dot_general(block, weight, (((1,), (1,)), ((), ())), preferred_elemen...  8.21 us
    concatenate x1, other arithmetic, body(): stacked = jnp.concatenate([gate_w[0], up_w[0]], axis=0)  6.21 us
    ppermute x1, waiting for transfers between devices, body(): taken = lax.ppermute(give, 'core', [(0, 1), (1, 0)])  4.79 us
  transfers between devices with their start and end apart: 8, of which 5 were waited for; matrix products, arithmetic and copies ran while one was open for 9% of the time, Pallas kernels for 0%

profile of v1, /device:TPU:6, one launch (start us, length us, event | category | flops | bytes accessed | tf_op | source)
XLA Modules:
  0.0 197.2 jit_solution(16559005471230070064)
XLA Ops:
  6.5 0.0 copy-start
  6.5 0.0 all-gather.2.cloned.1.call-start
  6.5 0.3 collective-permute-start
  6.8 0.7 collective-permute-start.1
  7.5 0.7 fusion.43
  8.2 1.3 fusion.38
  9.5 0.8 iota_compare_fusion.2
  10.3 0.0 collective-permute-done
  10.3 0.7 pad_add_fusion
  11.0 1.2 reduce-window.6
  12.2 0.1 slice.82
  12.2 0.1 copy.15
  12.4 0.1 fusion.20
  12.5 0.7 multiply_add_fusion
  13.2 0.6 fusion.65
  13.8 0.1 broadcast_compare_fusion
  13.9 0.0 collective-permute-done.1
  13.9 0.7 pad_clamp_fusion
  14.6 2.6 %gather_fusion = bf16[256,512]{1,0:T(8,128)(2,1)S(1)} fusion(bf16[1024,512]{1,0:T(8,128)(2,1)} %param.10, s32[1024]{0:T(1024)S(1)} %get-tuple-element.26), kind=kCustom, calls=%fused_computation | custom fusion | bytes 525312 | tf_op jit(solution)/shard_map/gather | solution.py:35
  17.2 1.3 convolution_convert_fusion.2
  18.7 30.5 %all_to_all.10 = bf16[16,1,32,512]{3,2,1,0:T(8,128)(2,1)S(1)} all-to-all(bf16[16,1,32,512]{3,2,1,0:T(8,128)(2,1)S(1)} %fusion.21), channel_id=1, replica_groups=mesh['chip'=8,'core'=2,'expert'=16] {'expert'}, dimensions={0} | all-to-all | bytes 1048576 | tf_op jit(solution)/shard_map/all_to_all | solution.py:76
  49.2 0.1 fusion.66
  49.2 0.1 slice_add_fusion
  49.3 0.1 fusion.64
  49.4 0.1 copy.25
  49.5 0.3 multiply_reduce_fusion
  49.8 0.9 multiply_convert_fusion.1
  50.7 0.0 all-gather.2.cloned.1.call-update
  50.7 0.0 reduce-scatter.2.cloned.1.call-start
  50.8 6.2 %pad_maximum_fusion = bf16[384,8192]{1,0:T(8,128)(2,1)} fusion(bf16[192,8192]{1,0:T(8,128)(2,1)} %bitcast.136, bf16[192,8192]{1,0:T(8,128)(2,1)} %bitcast.137), kind=kLoop, calls=%fused_computation.5 | loop fusion | flops 12582912 | bytes 12582912 | tf_op jit(solution)/shard_map/concatenate | solution.py:94
  57.0 1.0 collective-permute-start.2
  58.0 2.0 collective-permute-done.2
  59.9 30.8 %all-gather.2.cloned.1.call-done = bf16[384,8192]{1,0:T(8,128)(2,1)} async-done(((bf16[24,8192]{1,0:T(8,128)(2,1)}), bf16[384,8192]{1,0:T(8,128)(2,1)}) %all-gather.2.cloned.1.call-update) | async-done | bytes 6291472 | tf_op jit(solution)/shard_map/all_gather | solution.py:93
  90.7 8.2 %fusion.67 = f32[384,384]{0,1:T(8,128)S(1)} fusion(bf16[384,8192]{1,0:T(8,128)(2,1)} %all-gather.2.cloned.1.call-done, bf16[384,8192]{1,0:T(8,128)(2,1)} %pad_maximum_fusion), kind=kOutput, calls=%fused_computation.132 | convolution fusion | flops 2415919104 | bytes 13172736 | tf_op jit(solution)/shard_map/dot_general | solution.py:20
  98.9 0.1 fusion.7
  99.0 0.1 copy.19
  99.2 0.6 gather_fusion.1
  99.8 0.0 copy-done
  99.8 2.6 %convolution_convert_fusion = bf16[192,8192]{1,0:T(8,128)(2,1)} fusion(bf16[1,192,8192]{2,1,0:T(8,128)(2,1)S(1)} %copy-done, bf16[2,192,192]{2,1,0:T(8,128)(2,1)S(1)} %bitcast.141, s32[]{:T(128)S(6)} %select_n.116), kind=kOutput, calls=%fused_computation.3 | convolution fusion | flops 605552640 | bytes 6389764 | tf_op jit(solution)/shard_map/dot_general | solution.py:116
  102.4 0.2 collective-permute-start.4
  102.6 1.0 convolution_convert_fusion.1
  103.6 4.8 %collective-permute-done.4 = bf16[192,8192]{1,0:T(8,128)(2,1)} collective-permute-done((bf16[192,8192]{1,0:T(8,128)(2,1)}, bf16[192,8192]{1,0:T(8,128)(2,1)}, u32[]{:S(2)}, u32[]{:S(2)}) %collective-permute-start.4) | collective-permute-done | bytes 3145760 | tf_op jit(solution)/shard_map/ppermute | solution.py:124
  108.4 4.6 %add_convert_fusion = bf16[192,8192]{1,0:T(8,128)(2,1)} fusion(bf16[192,8192]{1,0:T(8,128)(2,1)} %collective-permute-done.4, bf16[192,8192]{1,0:T(8,128)(2,1)S(1)} %convolution_convert_fusion.1), kind=kLoop, calls=%fused_computation.6 | loop fusion | flops 6291456 | bytes 9437184 | tf_op jit(solution)/shard_map/convert_element_type | solution.py:126
  113.0 0.0 copy-start.1
  113.0 0.0 reduce-scatter.2.cloned.1.call-update
  113.1 0.5 collective-permute-start.3
  113.5 48.7 %reduce-scatter.2.cloned.1.call-done = bf16[24,8192]{1,0:T(8,128)(2,1)} async-done(((bf16[192,8192]{1,0:T(8,128)(2,1)}), bf16[24,8192]{1,0:T(8,128)(2,1)}) %reduce-scatter.2.cloned.1.call-update) | async-done | bytes 393232 | tf_op jit(solution)/shard_map/reduce_scatter | solution.py:127
  162.3 1.1 multiply_convert_fusion
  163.4 0.8 copy.31
  164.2 9.3 %all-to-all-start.1 = ((bf16[16,24,512]{2,1,0:T(8,128)(2,1)}), bf16[16,24,512]{2,1,0:T(8,128)(2,1)S(1)}, u32[]{:S(2)}, u32[]{:S(2)}) async-start(bf16[16,24,512]{2,1,0:T(8,128)(2,1)} %bitcast.139), calls=%async_computation.2 | async-start | bytes 786432 | tf_op jit(solution)/shard_map/all_to_all | solution.py:130
  173.5 0.0 copy-done.1
  173.5 1.6 scatter_custom_fusion
  175.1 11.9 %all-to-all-done.1 = bf16[16,24,512]{2,1,0:T(8,128)(2,1)S(1)} async-done(((bf16[16,24,512]{2,1,0:T(8,128)(2,1)}), bf16[16,24,512]{2,1,0:T(8,128)(2,1)S(1)}, u32[]{:S(2)}, u32[]{:S(2)}) %all-to-all-start.1) | async-done | bytes 393248 | tf_op jit(solution)/shard_map/all_to_all | solution.py:130
  187.0 0.8 fusion.2
  187.7 0.0 collective-permute-done.3
  187.8 2.6 %add_convert_fusion.1 = bf16[1024,512]{1,0:T(8,128)(2,1)} fusion(f32[1024,512]{1,0:T(8,128)S(1)} %fusion.2, bf16[1024,512]{1,0:T(8,128)(2,1)} %collective-permute-done.3), kind=kLoop, calls=%fused_computation.9 | loop fusion | flops 1572864 | bytes 4194304 | tf_op jit(solution)/shard_map/convert_element_type | solution.py:139
  (28 shorter events, 0.2 us)
Async XLA Ops:
  6.5 93.2 %copy-start = (bf16[1,192,8192]{2,1,0:T(8,128)(2,1)S(1)}, bf16[1,192,8192]{2,1,0:T(8,128)(2,1)}, u32[]{:S(2)}) copy-start(bf16[1,192,8192]{2,1,0:T(8,128)(2,1)} %param.17) | copy-start | bytes 9437188
  6.5 84.2 %all-gather.2.cloned.1.call-start = ((), (), s32[]{:S(2)}) async-start(), calls=%async_computation.3 | async-start | bytes 6684672 | tf_op jit(solution)/shard_map/all_gather | solution.py:93
  6.5 3.8 %collective-permute-start = (s32[256,1]{0,1:T(1,128)}, s32[256,1]{0,1:T(1,128)S(1)}, u32[]{:S(2)}, u32[]{:S(2)}) collective-permute-start(s32[256,1]{0,1:T(1,128)} %param.12), channel_id=1, source_target_pairs={{16,0},{32,16},{48,32},{64,48},{80,64},{96,80},{112,96},{128,112},... | collective-permute-start | bytes 3080 | tf_op jit(solution)/shard_map/ppermute | solution.py:16
  6.8 7.1 %collective-permute-start.1 = (s32[1,256]{1,0:T(1,128)}, s32[1,256]{1,0:T(1,128)S(1)}, u32[]{:S(2)}, u32[]{:S(2)}) collective-permute-start(s32[1,256]{1,0:T(1,128)} %param.11), channel_id=1, source_target_pairs={{16,0},{32,16},{48,32},{64,48},{80,64},{96,80},{112,96},{128,112},... | collective-permute-start | bytes 3080 | tf_op jit(solution)/shard_map/ppermute | solution.py:16
  50.7 111.6 %reduce-scatter.2.cloned.1.call-start = ((), (), s32[]{:S(2)}) async-start(), calls=%async_computation.4 | async-start | bytes 3538944 | tf_op jit(solution)/shard_map/reduce_scatter | solution.py:127
  57.0 3.0 %collective-permute-start.2 = (f32[24]{0:T(128)S(1)}, f32[24]{0:T(128)S(1)}, u32[]{:S(2)}, u32[]{:S(2)}) collective-permute-start(f32[24]{0:T(128)S(1)} %get-tuple-element.23), channel_id=1, source_target_pairs={{240,0},{0,16},{16,32},{32,48},{48,64},{64,80},{80,96},{96,112},{1... | collective-permute-start | bytes 296 | tf_op jit(solution)/shard_map/ppermute | solution.py:16
  102.4 6.0 %collective-permute-start.4 = (bf16[192,8192]{1,0:T(8,128)(2,1)}, bf16[192,8192]{1,0:T(8,128)(2,1)}, u32[]{:S(2)}, u32[]{:S(2)}) collective-permute-start(bf16[192,8192]{1,0:T(8,128)(2,1)} %convolution_convert_fusion), channel_id=1, source_target_pairs={{0,16},{16,0},{1,17},{17,1},{2,18},{18,2},{3,19},{19,3},{4,20},{20... | collective-permute-start | bytes 9437192 | tf_op jit(solution)/shard_map/ppermute | solution.py:124
  113.0 60.5 %copy-start.1 = (s32[1,256]{1,0:T(1,128)S(1)}, s32[1,256]{1,0:T(1,128)}, u32[]{:S(2)}) copy-start(s32[1,256]{1,0:T(1,128)} %param.11) | copy-start | bytes 3076
  113.1 74.7 %collective-permute-start.3 = (bf16[1024,512]{1,0:T(8,128)(2,1)}, bf16[1024,512]{1,0:T(8,128)(2,1)}, u32[]{:S(2)}, u32[]{:S(2)}) collective-permute-start(bf16[1024,512]{1,0:T(8,128)(2,1)} %param.10), channel_id=1, source_target_pairs={{240,0},{0,16},{16,32},{32,48},{48,64},{64,80},{80,96},{96,112},{1... | collective-permute-start | bytes 3145736 | tf_op jit(solution)/shard_map/ppermute | solution.py:16
  164.2 22.8 %all-to-all-start.1 = ((bf16[16,24,512]{2,1,0:T(8,128)(2,1)}), bf16[16,24,512]{2,1,0:T(8,128)(2,1)S(1)}, u32[]{:S(2)}, u32[]{:S(2)}) async-start(bf16[16,24,512]{2,1,0:T(8,128)(2,1)} %bitcast.139), calls=%async_computation.2 | async-start | bytes 786432 | tf_op jit(solution)/shard_map/all_to_all | solution.py:130
Sparse Core Ops, SparseCore 0:
  50.8 39.8 all-gather.1
  113.2 49.0 reduce-scatter.1
